TPU v7x, 512 devices: a whole 4x8x8 slice. The times are simulated.
512 devices in a mesh: dp: 4 (over y_hi, core), context: 16 (over y_lo, x), tensor: 8 (over z).
Axes of the slice: x: 4, y: 8 (y_hi: 2, y_lo: 4; y = y_hi * 4 + y_lo), z: 8, core: 2. Of those that a mesh axis runs over, the one named last changes fastest.
Arguments:
- queries: bfloat16 [8192, 4096], P(('dp', 'context'), 'tensor'), parts along dimension 0, may hold values from -6 to 6
- keys: bfloat16 [8192, 1024], P(('dp', 'context'), 'tensor'), parts along dimension 0, may hold values from -6 to 6
- values: bfloat16 [8192, 1024], P(('dp', 'context'), 'tensor'), parts along dimension 0, may hold values from -6 to 6
- order: int32 [8192], P('dp'), parts along dimension 0, may hold values from 0 to 2047, as said below
- out_weight: bfloat16 [4096, 4096], P('tensor', 'context'), may hold values from -0.125 to 0.125
Outputs:
- output: bfloat16 [8192, 4096], P(('dp', 'context'), 'tensor'), parts along dimension 0
There are 4 independent parts, one for each index of `dp`. A program takes and returns all parts, laid end to end along the dimension named above; an argument that names none is the same for every part. Nothing has to cross between parts.
Inputs may be any that keep to these rules, and one draw needn't show every extreme that they name: A permutation of the positions; each aligned block of 128 rows holds 128 consecutive positions in increasing order, starting at a multiple of 128.
All inputs are finite; a program needn't handle non-finite values.
Results may differ from a plain program's by a relative error of at most 0.019.
Values may be sent and summed in bfloat16 or wider, within the bound.
No kernel may reach another device: no remote copies, remote signals or barrier semaphores. Data moves between devices by JAX's collectives and lax.ppermute only.
A program may use at most 64 MiB of HBM per device.

v0:
```python
import math
import jax
import jax.numpy as jnp
from jax import lax
from jax.sharding import PartitionSpec as P

QUERY_HEADS = 32
KEY_VALUE_HEADS = 8
HEAD_SIZE = 128


def per_device(queries, keys, values, order, out_weight):
    row_count = queries.shape[0]
    local_groups = keys.shape[1] // HEAD_SIZE
    query_head_group = QUERY_HEADS // KEY_VALUE_HEADS
    score_scale = 1.0 / math.sqrt(HEAD_SIZE)
    first_row = lax.axis_index("context") * row_count
    query_pos = lax.dynamic_slice_in_dim(order, first_row, row_count, 0)
    stacked = queries.reshape(row_count, local_groups, query_head_group, HEAD_SIZE)
    stacked = stacked.transpose(1, 2, 0, 3).reshape(
        local_groups, query_head_group * row_count, HEAD_SIZE
    )
    stacked_pos = jnp.tile(query_pos, query_head_group)
    stacked_rows = query_head_group * row_count
    key_part = lax.all_gather(keys, "context", axis=0, tiled=True)
    value_part = lax.all_gather(values, "context", axis=0, tiled=True)
    key_count = key_part.shape[0]
    running_max = jnp.full((local_groups, stacked_rows), -1e30, jnp.float32)
    key_heads = key_part.reshape(key_count, local_groups, HEAD_SIZE)
    value_heads = value_part.reshape(key_count, local_groups, HEAD_SIZE)
    scores = (
        jnp.einsum("grd,kgd->grk", stacked, key_heads, preferred_element_type=jnp.float32)
        * score_scale
    )
    visible = order[None, None, :] <= stacked_pos[None, :, None]
    scores = jnp.where(visible, scores, -1e30)
    new_max = jnp.maximum(running_max, jnp.max(scores, axis=2))
    weights = jnp.where(visible, jnp.exp(scores - new_max[..., None]), 0.0)
    new_sum = jnp.sum(weights, axis=2)
    product = jnp.einsum(
        "grk,kgd->grd",
        weights.astype(jnp.bfloat16),
        value_heads,
        preferred_element_type=jnp.float32,
    )
    attended = (product / new_sum[..., None]).astype(jnp.bfloat16)
    attended = attended.reshape(local_groups, query_head_group, row_count, HEAD_SIZE).transpose(
        2, 0, 1, 3
    )
    attended = attended.reshape(row_count, local_groups * query_head_group * HEAD_SIZE)
    partial_out = jnp.dot(
        attended,
        lax.all_gather(out_weight, "context", axis=1, tiled=True),
        preferred_element_type=jnp.float32,
    )
    summed = lax.psum(partial_out.astype(jnp.bfloat16), "tensor").astype(jnp.float32)
    column_count = summed.shape[1] // lax.axis_size("tensor")
    mine = lax.dynamic_slice_in_dim(
        summed, lax.axis_index("tensor") * column_count, column_count, 1
    )
    return mine.astype(jnp.bfloat16)


def solution(mesh):
    placed = (
        P(("dp", "context"), "tensor"),
        P(("dp", "context"), "tensor"),
        P(("dp", "context"), "tensor"),
        P("dp"),
        P("tensor", "context"),
    )
    return jax.shard_map(
        per_device,
        mesh=mesh,
        in_specs=placed,
        out_specs=P(("dp", "context"), "tensor"),
        check_vma=False,
    )
```

profile of v0, /device:TPU:2, one launch (start us, length us, event | category | flops | bytes accessed | tf_op | source)
XLA Modules:
  0.0 208.4 jit_solution(8475246983671661402)
XLA Ops:
  6.5 0.0 copy-start.1
  6.5 0.0 copy-start
  6.5 0.0 all-gather.2.cloned.1.call-start
  6.5 0.7 all-gather.2.cloned.1.call-update
  7.3 0.0 all-reduce.2.cloned.1.call-start
  7.3 1.0 copy.7
  8.3 0.1 copy.8
  8.5 0.8 dynamic_slice.6
  9.3 47.2 %all_gather.9 = bf16[2048,128]{1,0:T(8,128)(2,1)S(1)} all-gather(bf16[128,128]{1,0:T(8,128)(2,1)} %param.6), channel_id=1, replica_groups=mesh['dp'=4,'context'=16,'tensor'=8] {'context'}, dimensions={0}, use_global_device_ids=true | all-gather | bytes 557056 | tf_op jit(solution)/shard_map/all_gather | solution.py:25
  56.4 1.6 fusion
  58.0 0.0 copy-done
  58.0 42.5 %all_gather.10 = bf16[2048,128]{1,0:T(8,128)(2,1)S(1)} all-gather(bf16[128,128]{1,0:T(8,128)(2,1)S(1)} %copy-done), channel_id=1, replica_groups=mesh['dp'=4,'context'=16,'tensor'=8] {'context'}, dimensions={0}, use_global_device_ids=true | all-gather | bytes 557056 | tf_op jit(solution)/shard_map/all_gather | solution.py:26
  100.5 0.0 copy-done.1
  100.5 1.2 fusion.1
  101.7 1.1 fusion.8
  102.9 0.1 copy.9
  103.0 6.5 %all-gather.2.cloned.1.call-done = bf16[512,4096]{1,0:T(8,128)(2,1)} async-done(((bf16[512,256]{1,0:T(8,128)(2,1)}), bf16[512,4096]{1,0:T(8,128)(2,1)}) %all-gather.2.cloned.1.call-update) | async-done | bytes 4194320 | tf_op jit(solution)/shard_map/all_gather | solution.py:53
  109.5 3.9 %convolution_convert_fusion = bf16[128,4096]{1,0:T(8,128)(2,1)} fusion(bf16[128,512]{0,1:T(8,128)(2,1)S(1)} %bitcast.16, bf16[512,4096]{1,0:T(8,128)(2,1)} %all-gather.2.cloned.1.call-done), kind=kOutput, calls=%fused_computation.2 | convolution fusion | flops 537395200 | bytes 5373952 | tf_op jit(solution)/shard_map/dot_general | solution.py:51
  113.5 0.0 all-reduce.2.cloned.1.call-update
  113.5 86.5 %all-reduce.2.cloned.1.call-done = bf16[128,4096]{1,0:T(8,128)(2,1)} async-done(((bf16[128,4096]{1,0:T(8,128)(2,1)}), bf16[128,4096]{1,0:T(8,128)(2,1)}) %all-reduce.2.cloned.1.call-update) | async-done | bytes 1048592 | tf_op jit(solution)/shard_map/psum | solution.py:56
  200.0 1.6 convert_convert_fusion
  (2 shorter events, 0.0 us)
Async XLA Ops:
  6.5 94.0 %copy-start.1 = (s32[2048]{0:T(1024)S(1)}, s32[2048]{0:T(1024)}, u32[]{:S(2)}) copy-start(s32[2048]{0:T(1024)} %param.8) | copy-start | bytes 24580
  6.5 51.5 %copy-start = (bf16[128,128]{1,0:T(8,128)(2,1)S(1)}, bf16[128,128]{1,0:T(8,128)(2,1)}, u32[]{:S(2)}) copy-start(bf16[128,128]{1,0:T(8,128)(2,1)} %param.7) | copy-start | bytes 98308
  6.5 103.0 %all-gather.2.cloned.1.call-start = ((), (), s32[]{:S(2)}) async-start(), calls=%async_computation | async-start | bytes 4456448 | tf_op jit(solution)/shard_map/all_gather | solution.py:53
  7.3 192.7 %all-reduce.2.cloned.1.call-start = ((), (), s32[]{:S(2)}) async-start(), calls=%async_computation.1 | async-start | bytes 2097152 | tf_op jit(solution)/shard_map/psum | solution.py:56
Sparse Core Ops, SparseCore 0:
  9.3 100.1 all-gather.1
  113.6 86.3 all-reduce.1
where the time goes:
time: 209 us; the launch traced here: 208 us
  waiting for transfers between devices  93.8 us (45%)
  blocking collectives  89.6 us (43%)
  between operations  13.4 us (6%)
  matrix products  6.62 us (3%)
  other arithmetic  2.82 us (1%)
    psum x1, waiting for transfers between devices, per_device(): lax.psum(partial_out.astype(jnp.bfloat16), 'tensor').astype(jnp.float32)  86.5 us
    all_gather x1, blocking collectives, per_device(): key_part = lax.all_gather(keys, 'context', axis=0, tiled=True)  47.2 us
    all_gather x1, blocking collectives, per_device(): value_part = lax.all_gather(values, 'context', axis=0, tiled=True)  42.5 us
    all_gather x1, waiting for transfers between devices, per_device(): lax.all_gather(out_weight, 'context', axis=1, tiled=True)  6.54 us
  transfers between devices with their start and end apart: 2, of which 2 were waited for; matrix products, arithmetic and copies ran while one was open for 3% of the time, Pallas kernels for 0%

commit v1 on v0

--- a/solution.py
+++ b/solution.py
@@ -53,7 +53,9 @@
         lax.all_gather(out_weight, "context", axis=1, tiled=True),
         preferred_element_type=jnp.float32,
     )
-    summed = lax.psum(partial_out.astype(jnp.bfloat16), "tensor").astype(jnp.float32)
+    summed = jnp.sum(lax.all_gather(partial_out.astype(jnp.bfloat16), "tensor"), axis=0).astype(
+        jnp.float32
+    )
     column_count = summed.shape[1] // lax.axis_size("tensor")
     mine = lax.dynamic_slice_in_dim(
         summed, lax.axis_index("tensor") * column_count, column_count, 1

time: 209 us -> 229 us (1.096)
  the two profiles are of different devices: /device:TPU:2 before, /device:TPU:1 now
where the time goes in v1:
time: 229 us; the launch traced here: 228 us
  waiting for transfers between devices  123 us (54%)
  blocking collectives  76.8 us (34%)
  between operations  13.5 us (6%)
  other arithmetic  6.83 us (3%)
  matrix products  6.72 us (3%)
    all_gather x1, waiting for transfers between devices, per_device(): lax.all_gather(partial_out.astype(jnp.bfloat16), 'tensor')  110 us
    all_gather x1, blocking collectives, per_device(): key_part = lax.all_gather(keys, 'context', axis=0, tiled=True)  40.2 us
    all_gather x1, blocking collectives, per_device(): value_part = lax.all_gather(values, 'context', axis=0, tiled=True)  36.6 us
    all_gather x1, waiting for transfers between devices, per_device(): lax.all_gather(out_weight, 'context', axis=1, tiled=True)  11.8 us
    reduce_sum x1, other arithmetic, per_device(): jnp.sum(lax.all_gather(partial_out.astype(jnp.bfloat16), 'tensor'), axis=0)  4.9 us
  transfers between devices with their start and end apart: 2, of which 2 were waited for; matrix products, arithmetic and copies ran while one was open for 3% of the time, Pallas kernels for 0%

profile of v1, /device:TPU:1, one launch (start us, length us, event | category | flops | bytes accessed | tf_op | source)
XLA Modules:
  0.0 228.4 jit_solution(8456694613087629323)
XLA Ops:
  6.5 0.0 copy-start.1
  6.5 0.0 copy-start
  6.5 0.0 all-gather.4.cloned.1.call-start
  6.5 0.7 all-gather.4.cloned.1.call-update
  7.3 0.0 all-gather.6.cloned.1.call-start
  7.3 1.0 copy.7
  8.3 0.1 copy.8
  8.5 0.8 dynamic_slice.6
  9.3 40.2 %all_gather.15 = bf16[2048,128]{1,0:T(8,128)(2,1)S(1)} all-gather(bf16[128,128]{1,0:T(8,128)(2,1)} %param.6), channel_id=1, replica_groups=mesh['dp'=4,'context'=16,'tensor'=8] {'context'}, dimensions={0}, use_global_device_ids=true | all-gather | bytes 557056 | tf_op jit(solution)/shard_map/all_gather | solution.py:25
  49.4 1.6 fusion
  51.1 0.0 copy-done
  51.1 36.6 %all_gather.16 = bf16[2048,128]{1,0:T(8,128)(2,1)S(1)} all-gather(bf16[128,128]{1,0:T(8,128)(2,1)S(1)} %copy-done), channel_id=1, replica_groups=mesh['dp'=4,'context'=16,'tensor'=8] {'context'}, dimensions={0}, use_global_device_ids=true | all-gather | bytes 557056 | tf_op jit(solution)/shard_map/all_gather | solution.py:26
  87.6 0.0 copy-done.1
  87.7 1.2 fusion.1
  88.9 1.1 fusion.8
  90.0 0.1 copy.9
  90.2 11.8 %all-gather.4.cloned.1.call-done = bf16[512,4096]{1,0:T(8,128)(2,1)} async-done(((bf16[512,256]{1,0:T(8,128)(2,1)}), bf16[512,4096]{1,0:T(8,128)(2,1)}) %all-gather.4.cloned.1.call-update) | async-done | bytes 4194320 | tf_op jit(solution)/shard_map/all_gather | solution.py:53
  102.0 4.0 %convolution_convert_fusion = bf16[128,4096]{1,0:T(8,128)(2,1)} fusion(bf16[128,512]{0,1:T(8,128)(2,1)S(1)} %bitcast.18, bf16[512,4096]{1,0:T(8,128)(2,1)} %all-gather.4.cloned.1.call-done), kind=kOutput, calls=%fused_computation.2 | convolution fusion | flops 537395200 | bytes 5373952 | tf_op jit(solution)/shard_map/dot_general | solution.py:51
  106.0 0.0 all-gather.6.cloned.1.call-update
  106.0 110.0 %all-gather.6.cloned.1.call-done = bf16[1024,4096]{1,0:T(8,128)(2,1)} async-done(((bf16[128,4096]{1,0:T(8,128)(2,1)}), bf16[1024,4096]{1,0:T(8,128)(2,1)}) %all-gather.6.cloned.1.call-update) | async-done | bytes 8388624 | tf_op jit(solution)/shard_map/all_gather | solution.py:56
  216.0 4.9 %reduce_sum.22 = bf16[128,4096]{1,0:T(8,128)(2,1)S(1)} reduce(bf16[8,128,4096]{2,1,0:T(8,128)(2,1)} %bitcast.16, bf16[]{:T(256)} %constant.26.clone.1), dimensions={0}, to_apply=%region_2.3 | reduce | flops 3670016 | bytes 9437186 | tf_op jit(solution)/shard_map/reduce_sum | solution.py:56
  220.9 0.7 convert_convert_fusion
  (2 shorter events, 0.0 us)
Async XLA Ops:
  6.5 81.1 %copy-start.1 = (s32[2048]{0:T(1024)S(1)}, s32[2048]{0:T(1024)}, u32[]{:S(2)}) copy-start(s32[2048]{0:T(1024)} %param.8) | copy-start | bytes 24580
  6.5 44.5 %copy-start = (bf16[128,128]{1,0:T(8,128)(2,1)S(1)}, bf16[128,128]{1,0:T(8,128)(2,1)}, u32[]{:S(2)}) copy-start(bf16[128,128]{1,0:T(8,128)(2,1)} %param.7) | copy-start | bytes 98308
  6.5 95.4 %all-gather.4.cloned.1.call-start = ((), (), s32[]{:S(2)}) async-start(), calls=%async_computation | async-start | bytes 4456448 | tf_op jit(solution)/shard_map/all_gather | solution.py:53
  7.3 208.7 %all-gather.6.cloned.1.call-start = ((), (), s32[]{:S(2)}) async-start(), calls=%async_computation.1 | async-start | bytes 9437184 | tf_op jit(solution)/shard_map/all_gather | solution.py:56
Sparse Core Ops, SparseCore 0:
  9.3 92.5 all-gather.3
  106.1 109.8 all-gather.5
